TPU v7x, 256 devices: a whole 4x4x8 slice. The times are simulated.
256 devices in a mesh: lat: 16 (over x_hi, y, core), lon: 16 (over z, x_lo).
Axes of the slice: x: 4 (x_hi: 2, x_lo: 2; x = x_hi * 2 + x_lo), y: 4, z: 8, core: 2. Of those that a mesh axis runs over, the one named last changes fastest.
Arguments:
- initial: float32 [64, 256, 2048], P(None, 'lat', 'lon'), may hold values from -6 to 6
- east_wind: float32 [64, 256, 2048], P(None, 'lat', 'lon'), may hold values from -2.5 to 2.5
- north_wind: float32 [64, 256, 2048], P(None, 'lat', 'lon'), may hold values from -2.5 to 2.5
- east_mask: int32 [64, 256, 2048], P(None, 'lat', 'lon'), may hold values from 0 to 1
- north_mask: int32 [64, 256, 2048], P(None, 'lat', 'lon'), may hold values from 0 to 1
- mixing: float32 [63], replicated, may hold values from 0.02 to 0.2
- obs_cell: int32 [16, 16, 4, 256], P('lat', 'lon'), may hold values from 0 to 2047
- obs_level: int32 [16, 16, 4, 256], P('lat', 'lon'), may hold values from 0 to 63
- obs_value: float32 [16, 16, 4, 256], P('lat', 'lon'), may hold values from -6 to 6
- obs_weight: float32 [16, 16, 4, 256], P('lat', 'lon'), may hold values from 0.2 to 2
Outputs:
- gradient: float32 [64, 256, 2048], P(None, 'lat', 'lon')
- cost: float32 [], replicated
Inputs may be any that keep to these rules, and one draw needn't show every extreme that they name: `obs_cell`: row times 128 plus column within the block.
All inputs are finite; a program needn't handle non-finite values.
Results may differ from a plain program's by a relative error of at most 0.0003.
Values sent between devices are 32-bit elements; how exact they have to be, the bound alone decides.
No kernel may reach another device: no remote copies, remote signals or barrier semaphores. Data moves between devices by JAX's collectives and lax.ppermute only.
A program may use at most 64 MiB of HBM per device.

v0:
```python
import jax
import jax.numpy as jnp
from jax import lax
from jax.sharding import PartitionSpec as P

STEPS = 4
HALO = STEPS


def face_parts(velocity, branch):
    share = jnp.where(branch == 1, jnp.where(velocity > 0, 1.0, 0.0), 0.5)
    return (velocity * share, velocity * (1.0 - share))


def vertical(field, mixing):
    flux = mixing[:, None, None] * (field[1:] - field[:-1])
    zero_row = jnp.zeros_like(field[:1])
    return jnp.concatenate([flux, zero_row], 0) - jnp.concatenate([zero_row, flux], 0)


def shift(x, offset, dim):
    pad = [(0, 0)] * x.ndim
    size = x.shape[dim]
    if offset > 0:
        pad[dim] = (offset, 0)
        return lax.slice_in_dim(jnp.pad(x, pad), 0, size, axis=dim)
    pad[dim] = (0, -offset)
    return lax.slice_in_dim(jnp.pad(x, pad), -offset, size - offset, axis=dim)


def ring(axis, periodic):
    count = lax.axis_size(axis)
    up = [(i, i + 1) for i in range(count - 1)]
    if periodic:
        up.append((count - 1, 0))
    down = [(t, s) for s, t in up]
    return up, down


def grow(block, axis, width, dim, periodic):
    up, down = ring(axis, periodic)
    size = block.shape[dim]
    low = lax.ppermute(lax.slice_in_dim(block, size - width, size, axis=dim), axis, up)
    high = lax.ppermute(lax.slice_in_dim(block, 0, width, axis=dim), axis, down)
    return jnp.concatenate([low, block, high], axis=dim)


def fold(block, axis, width, dim, periodic, value):
    up, down = ring(axis, periodic)
    size = block.shape[dim]
    slab = jnp.broadcast_to(value, (1,) + tuple(n if d != dim else width for d, n in enumerate(block.shape[1:], 1)))
    top = jnp.concatenate([lax.slice_in_dim(block, size - width, size, axis=dim), slab], 0)
    bottom = jnp.concatenate([lax.slice_in_dim(block, 0, width, axis=dim), slab], 0)
    from_high = lax.ppermute(top, axis, up)
    from_low = lax.ppermute(bottom, axis, down)
    levels = block.shape[0]
    odd = lax.axis_index(axis) % 2 == 1
    partner = jnp.where(odd, from_high[levels].reshape(-1)[0], from_low[levels].reshape(-1)[0])
    from_high = from_high[:levels]
    from_low = from_low[:levels]
    inner = lax.slice_in_dim(block, width, size - width, axis=dim)
    n = inner.shape[dim]
    pad_lo = [(0, 0)] * block.ndim
    pad_hi = [(0, 0)] * block.ndim
    pad_lo[dim] = (0, n - width)
    pad_hi[dim] = (n - width, 0)
    return inner + jnp.pad(from_high, pad_lo) + jnp.pad(from_low, pad_hi), value + partner


def total(value, axes, first):
    for axis in axes:
        count = lax.axis_size(axis)
        step = first
        while step < count:
            pairs = [(i, i ^ step) for i in range(count)]
            value = value + lax.ppermute(value, axis, pairs)
            step *= 2
    return value


def on_device(
    initial,
    east_wind,
    north_wind,
    east_mask,
    north_mask,
    mixing,
    obs_cell,
    obs_level,
    obs_value,
    obs_weight,
):
    levels, rows, cols = initial.shape
    h = HALO
    west_p, west_q = face_parts(east_wind, east_mask)
    south_p, south_q = face_parts(north_wind, north_mask)
    global_row = lax.axis_index("lat") * rows + lax.iota(jnp.int32, rows)
    keep = (global_row > 0)[None, :, None]
    south_p = jnp.where(keep, south_p, 0.0)
    south_q = jnp.where(keep, south_q, 0.0)

    fields = jnp.stack([initial, west_p, west_q, south_p, south_q])
    fields = grow(fields, "lat", h, 2, False)
    fields = grow(fields, "lon", h, 3, True)

    state = fields[0]
    px, qx, py, qy = fields[1], fields[2], fields[3], fields[4]
    pxe = shift(px, -1, 2)
    qxe = shift(qx, -1, 2)
    pyn = shift(py, -1, 1)
    qyn = shift(qy, -1, 1)
    centre = (pxe - qx) + (pyn - qy)

    def forward_step(x):
        west = shift(x, 1, 2)
        east = shift(x, -1, 2)
        south = shift(x, 1, 1)
        north = shift(x, -1, 1)
        flow = centre * x + qxe * east - px * west + qyn * north - py * south
        return x + vertical(x, mixing) - flow

    def reverse_step(a):
        west = shift(a, 1, 2)
        east = shift(a, -1, 2)
        south = shift(a, 1, 1)
        north = shift(a, -1, 1)
        back = -centre * a - qx * west + pxe * east - qy * south + pyn * north
        return a + vertical(a, mixing) + back

    flat = obs_level[0, 0] * (rows * cols) + obs_cell[0, 0]
    local_cost = jnp.zeros((), jnp.float32)
    injections = []
    for step in range(STEPS):
        state = forward_step(state)
        inner = state[:, h : h + rows, h : h + cols]
        innovation = inner.reshape(-1)[flat[step]] - obs_value[0, 0, step]
        weighted = obs_weight[0, 0, step] * innovation
        local_cost = local_cost + 0.5 * jnp.sum(weighted * innovation)
        injections.append(weighted)
    block = levels * rows * cols
    spots = jnp.arange(STEPS, dtype=jnp.int32)[:, None] * block + flat
    injected = jnp.zeros((STEPS * block,), jnp.float32).at[spots].add(jnp.stack(injections))
    injected = injected.reshape(STEPS, levels, rows, cols)
    injections = [jnp.pad(injected[k], ((0, 0), (h, h), (h, h))) for k in range(STEPS)]
    adjoint = jnp.zeros_like(injections[0])
    for step in range(STEPS - 1, -1, -1):
        adjoint = reverse_step(adjoint + injections[step])
    adjoint, value = fold(adjoint, "lon", h, 2, True, local_cost)
    gradient, value = fold(adjoint, "lat", h, 1, False, value)
    cost = total(value, ("lon", "lat"), 2)
    return (gradient, cost)


def solution(mesh):
    placed = (
        P(None, "lat", "lon"),
        P(None, "lat", "lon"),
        P(None, "lat", "lon"),
        P(None, "lat", "lon"),
        P(None, "lat", "lon"),
        P(),
        P("lat", "lon", None, None),
        P("lat", "lon", None, None),
        P("lat", "lon", None, None),
        P("lat", "lon", None, None),
    )
    return jax.shard_map(
        on_device,
        mesh=mesh,
        in_specs=placed,
        out_specs=(P(None, "lat", "lon"), P()),
        check_vma=False,
    )
```

profile of v0, /device:TPU:6, one launch (start us, length us, event | category | flops | bytes accessed | tf_op | source)
XLA Modules:
  0.0 194.7 jit_solution(3215130250746055791)
XLA Ops:
  9.8 5.2 %collective-permute-start.1 = (f32[5,64,4,128]{3,2,1,0:T(4,128)S(1)}, f32[5,64,4,128]{3,2,1,0:T(4,128)S(1)}, u32[]{:S(2)}, u32[]{:S(2)}) collective-permute-start(f32[5,64,4,128]{3,2,1,0:T(4,128)S(1)} %get-tuple-element.20), channel_id=1, source_target_pairs={{16,0},{32,16},{48,32},{64,48},{80,64},{96,80},{112,96},{128,112},... | collective-permute-start | bytes 1966088 | tf_op jit(solution)/shard_map/ppermute | solution.py:44
  17.1 6.0 %collective-permute-done.1 = f32[5,64,4,128]{3,2,1,0:T(4,128)S(1)} collective-permute-done((f32[5,64,4,128]{3,2,1,0:T(4,128)S(1)}, f32[5,64,4,128]{3,2,1,0:T(4,128)S(1)}, u32[]{:S(2)}, u32[]{:S(2)}) %collective-permute-start.1) | collective-permute-done | bytes 655392 | tf_op jit(solution)/shard_map/ppermute | solution.py:44
  23.1 7.4 %collective-permute-done = f32[5,64,4,128]{3,2,1,0:T(4,128)S(1)} collective-permute-done((f32[5,64,4,128]{3,2,1,0:T(4,128)S(1)}, f32[5,64,4,128]{3,2,1,0:T(4,128)S(1)}, u32[]{:S(2)}, u32[]{:S(2)}) %collective-permute-start) | collective-permute-done | bytes 655392 | tf_op jit(solution)/shard_map/ppermute | solution.py:43
  31.2 4.3 %fusion.69 = (f32[5,64,24,4]{3,2,1,0:T(8,128)}, f32[5,64,24,4]{3,2,1,0:T(8,128)}) fusion(f32[5,64,24,128]{3,2,1,0:T(8,128)S(1)} %pad_maximum_fusion.1), kind=kLoop, calls=%fused_computation.160 | loop fusion | bytes 491520 | tf_op jit(solution)/shard_map/slice | solution.py:43
  35.5 3.4 %copy.25 = f32[5,64,24,4]{1,2,3,0:T(8,128)S(1)} copy(f32[5,64,24,4]{3,2,1,0:T(8,128)} %get-tuple-element.18) | data formatting | bytes 245760 | tf_op jit(solution)/shard_map/slice | solution.py:44
  39.0 3.4 %copy.24 = f32[5,64,24,4]{1,2,3,0:T(8,128)S(1)} copy(f32[5,64,24,4]{3,2,1,0:T(8,128)} %get-tuple-element.17) | data formatting | bytes 245760 | tf_op jit(solution)/shard_map/slice | solution.py:43
  42.4 3.2 %collective-permute-start.2 = (f32[5,64,24,4]{1,2,3,0:T(8,128)S(1)}, f32[5,64,24,4]{1,2,3,0:T(8,128)S(1)}, u32[]{:S(2)}, u32[]{:S(2)}) collective-permute-start(f32[5,64,24,4]{1,2,3,0:T(8,128)S(1)} %copy.24), channel_id=1, source_target_pairs={{0,1},{1,2},{2,3},{3,4},{4,5},{5,6},{6,7},{7,8},{8,9},{9,10},{10,1... | collective-permute-start | bytes 368648 | tf_op jit(solution)/shard_map/ppermute | solution.py:43
  49.0 5.1 %collective-permute-done.2 = f32[5,64,24,4]{1,2,3,0:T(8,128)S(1)} collective-permute-done((f32[5,64,24,4]{1,2,3,0:T(8,128)S(1)}, f32[5,64,24,4]{1,2,3,0:T(8,128)S(1)}, u32[]{:S(2)}, u32[]{:S(2)}) %collective-permute-start.2) | collective-permute-done | bytes 122912 | tf_op jit(solution)/shard_map/ppermute | solution.py:43
  57.0 8.3 %pad_maximum_fusion = f32[5,64,24,136]{3,2,1,0:T(8,128)S(1)} fusion(f32[5,64,24,4]{3,2,1,0:T(8,128)} %copy.27, f32[5,64,4,128]{3,2,1,0:T(4,128)S(1)} %collective-permute-done.1, f32[5,64,16,128]{3,2,1,0:T(8,128)} %bitcast_dynamic-update-slice_fusion, f32[5,64,4,128]{3,2,1,0:T(4,128)S(1)} %collective-permute-done, f32[5,64,24,4]{3,2,1,0:T(8,128)} %copy.26), kind=kLoop, calls=%fused_computation.5 | loop fusion | flops 4177920 | bytes 8355840 | tf_op jit(solution)/shard_map/concatenate | solution.py:45
  67.5 4.0 %fusion.9 = (f32[64,24,136]{2,1,0:T(8,128)S(1)}, f32[64,24,136]{2,1,0:T(8,128)S(1)}, f32[64,24,136]{2,1,0:T(8,128)}, f32[64,24,136]{2,1,0:T(8,128)}) fusion(f32[64,24,136]{2,1,0:T(8,128)S(1)} %get-tuple-element.16, f32[63,24,136]{2,1,0:T(8,128)S(1)} %fusion.49, f32[5,64,24,136]{3,2,1,0:T(8,128)S(1)} %pad_maximum_fusion, ...), kind=kLoop, calls=%fused_computation.38 | loop fusion | flops 3133440 | bytes 11685120 | tf_op jit(solution)/shard_map/sub | solution.py:120
  78.5 3.5 %pad_slice_fusion.21 = (f32[64,24,136]{2,1,0:T(8,128)}, f32[64,24,136]{2,1,0:T(8,128)}, f32[64,24,136]{2,1,0:T(8,128)}, f32[64,24,136]{2,1,0:T(8,128)}) fusion(f32[64,24,136]{2,1,0:T(8,128)S(1)} %fusion.19), kind=kLoop, calls=%fused_computation.75 | loop fusion | bytes 4177920 | tf_op jit(solution)/shard_map/slice | solution.py:28
  83.4 3.5 %gather_fusion = f32[256]{0:T(256)S(1)} fusion(f32[131072]{0:T(1024)} %bitcast.152, s32[1024]{0:T(1024)S(1)} %get-tuple-element.56), kind=kCustom, calls=%fused_computation | custom fusion | bytes 3072 | tf_op jit(solution)/shard_map/gather | solution.py:136
  86.9 3.5 %gather_fusion.1 = f32[256]{0:T(256)S(1)} fusion(f32[131072]{0:T(1024)} %bitcast.153, s32[1024]{0:T(1024)S(1)} %get-tuple-element.55), kind=kCustom, calls=%fused_computation.1 | custom fusion | bytes 3072 | tf_op jit(solution)/shard_map/gather | solution.py:136
  90.4 8.1 %fusion.73 = (f32[64,16,128]{2,1,0:T(8,128)}, f32[64,16,128]{2,1,0:T(8,128)}) fusion(f32[64,24,136]{2,1,0:T(8,128)} %copy-done.3, f32[64,24,136]{2,1,0:T(8,128)} %get-tuple-element.33, f32[64,24,136]{2,1,0:T(8,128)} %copy-done.1, f32[64,24,136]{2,1,0:T(8,128)} %get-tuple-element.32, f32[64,24,136]{2,1,0:T(8,128)} %get-tuple-element.30, ...), kind=kLoop, calls=%fused_computation.164 | loop fusion | flops 1572864 | bytes 7113984 | tf_op jit(solution)/shard_map/slice | solution.py:135
  98.5 3.5 %gather_fusion.2 = f32[256]{0:T(256)S(1)} fusion(f32[131072]{0:T(1024)} %bitcast.151, s32[1024]{0:T(1024)S(1)} %get-tuple-element.54), kind=kCustom, calls=%fused_computation.2 | custom fusion | bytes 3072 | tf_op jit(solution)/shard_map/gather | solution.py:136
  102.0 3.3 %gather_fusion.3 = f32[256]{0:T(256)S(1)} fusion(f32[131072]{0:T(1024)} %bitcast.150, s32[1024]{0:T(1024)S(1)} %get-tuple-element.53), kind=kCustom, calls=%fused_computation.3 | custom fusion | bytes 3072 | tf_op jit(solution)/shard_map/gather | solution.py:136
  105.3 7.4 %scatter_custom_fusion = f32[524288]{0:T(1024)} fusion(s32[1024]{0:T(1024)S(1)} %bitcast.163, f32[1024]{0:T(1024)S(1)} %bitcast.164, f32[]{:T(128)} %constant.15.clone.1), kind=kCustom, calls=%fused_computation.96 | custom fusion | flops 1024 | bytes 2097156 | tf_op jit(solution)/shard_map/scatter-add | solution.py:142
  115.8 4.1 %fusion.1 = f32[64,24,136]{2,1,0:T(8,128)S(1)} fusion(f32[64,16,128]{2,1,0:T(8,128)S(1)} %bitcast.149, f32[64,24,136]{2,1,0:T(8,128)S(1)} %pad.181, f32[64,16,128]{2,1,0:T(8,128)S(1)} %bitcast.156, f32[63,24,136]{2,1,0:T(8,128)S(1)} %fusion.41, f32[64,24,136]{2,1,0:T(8,128)S(1)} %get-tuple-element.5, f32[64,24,136]{2,1,0:T(8,128)S(1)} %get-tuple-element.12, ...), kind=kLoop, calls=%fused_computation.30 | loop fusion | flops 2924544 | bytes 7720192 | tf_op jit(solution)/shard_map/add | solution.py:147
  134.5 4.2 %collective-permute-start.5 = (f32[65,24,4]{0,1,2:T(8,128)S(1)}, f32[65,24,4]{0,1,2:T(8,128)S(1)}, u32[]{:S(2)}, u32[]{:S(2)}) collective-permute-start(f32[65,24,4]{0,1,2:T(8,128)S(1)} %concatenate.85.clone), channel_id=1, source_target_pairs={{1,0},{2,1},{3,2},{4,3},{5,4},{6,5},{7,6},{8,7},{9,8},{10,9},{11,1... | collective-permute-start | bytes 74888 | tf_op jit(solution)/shard_map/ppermute | solution.py:55
  148.2 7.3 %collective-permute-start.7 = (f32[65,4,128]{2,1,0:T(4,128)S(1)}, f32[65,4,128]{2,1,0:T(4,128)S(1)}, u32[]{:S(2)}, u32[]{:S(2)}) collective-permute-start(f32[65,4,128]{2,1,0:T(4,128)S(1)} %concatenate.87), channel_id=1, source_target_pairs={{16,0},{32,16},{48,32},{64,48},{80,64},{96,80},{112,96},{128,112},... | collective-permute-start | bytes 399368 | tf_op jit(solution)/shard_map/ppermute | solution.py:55
  165.4 3.3 %collective-permute-done.9 = f32[]{:T(128)} collective-permute-done((f32[]{:T(128)}, f32[]{:T(128)}, u32[]{:S(2)}, u32[]{:S(2)}) %collective-permute-start.9) | collective-permute-done | bytes 36 | tf_op jit(solution)/shard_map/ppermute | solution.py:76
  172.1 4.8 %collective-permute-done.10 = f32[]{:T(128)} collective-permute-done((f32[]{:T(128)}, f32[]{:T(128)}, u32[]{:S(2)}, u32[]{:S(2)}) %collective-permute-start.10) | collective-permute-done | bytes 36 | tf_op jit(solution)/shard_map/ppermute | solution.py:76
  183.2 3.9 %collective-permute-done.12 = f32[]{:T(128)} collective-permute-done((f32[]{:T(128)}, f32[]{:T(128)}, u32[]{:S(2)}, u32[]{:S(2)}) %collective-permute-start.12) | collective-permute-done | bytes 36 | tf_op jit(solution)/shard_map/ppermute | solution.py:76
  189.1 3.9 %collective-permute-done.13 = f32[]{:T(128)} collective-permute-done((f32[]{:T(128)}, f32[]{:T(128)}, u32[]{:S(2)}, u32[]{:S(2)}) %collective-permute-start.13) | collective-permute-done | bytes 36 | tf_op jit(solution)/shard_map/ppermute | solution.py:76
  (123 shorter events, 70.5 us)
Async XLA Ops:
  6.8 10.2 %copy-start.15 = (s32[1,1,4,256]{3,2,1,0:T(4,128)S(1)}, s32[1,1,4,256]{3,2,1,0:T(4,128)}, u32[]{:S(2)}) copy-start(s32[1,1,4,256]{3,2,1,0:T(4,128)} %param.16) | copy-start | bytes 12292
  6.8 10.3 %copy-start.16 = (s32[1,1,4,256]{3,2,1,0:T(4,128)S(1)}, s32[1,1,4,256]{3,2,1,0:T(4,128)}, u32[]{:S(2)}) copy-start(s32[1,1,4,256]{3,2,1,0:T(4,128)} %param.17) | copy-start | bytes 12292
  7.7 9.4 %copy-start.14 = (f32[1,1,4,256]{3,2,1,0:T(4,128)S(1)}, f32[1,1,4,256]{3,2,1,0:T(4,128)}, u32[]{:S(2)}) copy-start(f32[1,1,4,256]{3,2,1,0:T(4,128)} %param.19) | copy-start | bytes 12292
  7.7 9.4 %copy-start.13 = (f32[1,1,4,256]{3,2,1,0:T(4,128)S(1)}, f32[1,1,4,256]{3,2,1,0:T(4,128)}, u32[]{:S(2)}) copy-start(f32[1,1,4,256]{3,2,1,0:T(4,128)} %param.18) | copy-start | bytes 12292
  7.7 22.8 %copy-start.4 = (f32[5,64,16,128]{3,2,1,0:T(8,128)S(1)}, f32[5,64,16,128]{3,2,1,0:T(8,128)}, u32[]{:S(2)}) copy-start(f32[5,64,16,128]{3,2,1,0:T(8,128)} %bitcast_dynamic-update-slice_fusion) | copy-start | bytes 7864324
  9.8 13.3 %collective-permute-start.1 = (f32[5,64,4,128]{3,2,1,0:T(4,128)S(1)}, f32[5,64,4,128]{3,2,1,0:T(4,128)S(1)}, u32[]{:S(2)}, u32[]{:S(2)}) collective-permute-start(f32[5,64,4,128]{3,2,1,0:T(4,128)S(1)} %get-tuple-element.20), channel_id=1, source_target_pairs={{16,0},{32,16},{48,32},{64,48},{80,64},{96,80},{112,96},{128,112},... | collective-permute-start | bytes 1966088 | tf_op jit(solution)/shard_map/ppermute | solution.py:44
  15.1 15.5 %collective-permute-start = (f32[5,64,4,128]{3,2,1,0:T(4,128)S(1)}, f32[5,64,4,128]{3,2,1,0:T(4,128)S(1)}, u32[]{:S(2)}, u32[]{:S(2)}) collective-permute-start(f32[5,64,4,128]{3,2,1,0:T(4,128)S(1)} %get-tuple-element.19), channel_id=1, source_target_pairs={{0,16},{16,32},{32,48},{48,64},{64,80},{80,96},{96,112},{112,128},... | collective-permute-start | bytes 1966088 | tf_op jit(solution)/shard_map/ppermute | solution.py:43
  38.9 7.3 %collective-permute-start.3 = (f32[5,64,24,4]{1,2,3,0:T(8,128)S(1)}, f32[5,64,24,4]{1,2,3,0:T(8,128)S(1)}, u32[]{:S(2)}, u32[]{:S(2)}) collective-permute-start(f32[5,64,24,4]{1,2,3,0:T(8,128)S(1)} %copy.25), channel_id=1, source_target_pairs={{1,0},{2,1},{3,2},{4,3},{5,4},{6,5},{7,6},{8,7},{9,8},{10,9},{11,1... | collective-permute-start | bytes 368648 | tf_op jit(solution)/shard_map/ppermute | solution.py:44
  42.4 11.7 %collective-permute-start.2 = (f32[5,64,24,4]{1,2,3,0:T(8,128)S(1)}, f32[5,64,24,4]{1,2,3,0:T(8,128)S(1)}, u32[]{:S(2)}, u32[]{:S(2)}) collective-permute-start(f32[5,64,24,4]{1,2,3,0:T(8,128)S(1)} %copy.24), channel_id=1, source_target_pairs={{0,1},{1,2},{2,3},{3,4},{4,5},{5,6},{6,7},{7,8},{8,9},{9,10},{10,1... | collective-permute-start | bytes 368648 | tf_op jit(solution)/shard_map/ppermute | solution.py:43
  65.3 10.9 %copy-start = (f32[5,64,24,136]{3,2,1,0:T(8,128)}, f32[5,64,24,136]{3,2,1,0:T(8,128)S(1)}, u32[]{:S(2)}) copy-start(f32[5,64,24,136]{3,2,1,0:T(8,128)S(1)} %pad_maximum_fusion) | copy-start | bytes 12533764
  115.8 4.4 %slice-start = ((s8[7864320]{0:T(1024)(128)(4,1)}), s8[4194304]{0:T(1024)(128)(4,1)S(1)}, s32[]{:S(2)}) async-start(s8[7864320]{0:T(1024)(128)(4,1)} %bitcast.145), calls=%async_computation | async-start | bytes 8388608
  115.8 4.4 %slice-start.1 = ((s8[7864320]{0:T(1024)(128)(4,1)}), s8[3670016]{0:T(1024)(128)(4,1)S(1)}, s32[]{:S(2)}) async-start(s8[7864320]{0:T(1024)(128)(4,1)} %bitcast.145), calls=%async_computation.1 | async-start | bytes 7340032
  129.4 14.4 %copy-start.6 = (f32[64,24,136]{2,1,0:T(8,128)S(1)}, f32[64,24,136]{2,1,0:T(8,128)}, u32[]{:S(2)}) copy-start(f32[64,24,136]{2,1,0:T(8,128)} %copy-done.5) | copy-start | bytes 2506756
  134.5 6.0 %collective-permute-start.5 = (f32[65,24,4]{0,1,2:T(8,128)S(1)}, f32[65,24,4]{0,1,2:T(8,128)S(1)}, u32[]{:S(2)}, u32[]{:S(2)}) collective-permute-start(f32[65,24,4]{0,1,2:T(8,128)S(1)} %concatenate.85.clone), channel_id=1, source_target_pairs={{1,0},{2,1},{3,2},{4,3},{5,4},{6,5},{7,6},{8,7},{9,8},{10,9},{11,1... | collective-permute-start | bytes 74888 | tf_op jit(solution)/shard_map/ppermute | solution.py:55
  139.0 4.4 %collective-permute-start.4 = (f32[65,24,4]{0,1,2:T(8,128)S(1)}, f32[65,24,4]{0,1,2:T(8,128)S(1)}, u32[]{:S(2)}, u32[]{:S(2)}) collective-permute-start(f32[65,24,4]{0,1,2:T(8,128)S(1)} %concatenate.84.clone), channel_id=1, source_target_pairs={{0,1},{1,2},{2,3},{3,4},{4,5},{5,6},{6,7},{7,8},{8,9},{9,10},{10,1... | collective-permute-start | bytes 74888 | tf_op jit(solution)/shard_map/ppermute | solution.py:54
  145.2 16.0 %copy-start.8 = (f32[64,24,128]{2,1,0:T(8,128)S(1)}, f32[64,24,128]{2,1,0:T(8,128)}, u32[]{:S(2)}) copy-start(f32[64,24,128]{2,1,0:T(8,128)} %copy-done.7) | copy-start | bytes 2359300
  146.2 9.9 %collective-permute-start.6 = (f32[65,4,128]{2,1,0:T(4,128)S(1)}, f32[65,4,128]{2,1,0:T(4,128)S(1)}, u32[]{:S(2)}, u32[]{:S(2)}) collective-permute-start(f32[65,4,128]{2,1,0:T(4,128)S(1)} %concatenate.86), channel_id=1, source_target_pairs={{0,16},{16,32},{32,48},{48,64},{64,80},{80,96},{96,112},{112,128},... | collective-permute-start | bytes 399368 | tf_op jit(solution)/shard_map/ppermute | solution.py:54
  148.2 9.8 %collective-permute-start.7 = (f32[65,4,128]{2,1,0:T(4,128)S(1)}, f32[65,4,128]{2,1,0:T(4,128)S(1)}, u32[]{:S(2)}, u32[]{:S(2)}) collective-permute-start(f32[65,4,128]{2,1,0:T(4,128)S(1)} %concatenate.87), channel_id=1, source_target_pairs={{16,0},{32,16},{48,32},{64,48},{80,64},{96,80},{112,96},{128,112},... | collective-permute-start | bytes 399368 | tf_op jit(solution)/shard_map/ppermute | solution.py:55
  159.8 3.6 %collective-permute-start.8 = (f32[]{:T(128)}, f32[]{:T(128)}, u32[]{:S(2)}, u32[]{:S(2)}) collective-permute-start(f32[]{:T(128)} %add.427), channel_id=1, source_target_pairs={{0,2},{1,3},{2,0},{3,1},{4,6},{5,7},{6,4},{7,5},{8,10},{9,11},{10,... | collective-permute-start | bytes 20 | tf_op jit(solution)/shard_map/ppermute | solution.py:76
  164.1 4.7 %collective-permute-start.9 = (f32[]{:T(128)}, f32[]{:T(128)}, u32[]{:S(2)}, u32[]{:S(2)}) collective-permute-start(f32[]{:T(128)} %add.428), channel_id=1, source_target_pairs={{0,4},{1,5},{2,6},{3,7},{4,0},{5,1},{6,2},{7,3},{8,12},{9,13},{10,... | collective-permute-start | bytes 20 | tf_op jit(solution)/shard_map/ppermute | solution.py:76
  169.3 7.7 %collective-permute-start.10 = (f32[]{:T(128)}, f32[]{:T(128)}, u32[]{:S(2)}, u32[]{:S(2)}) collective-permute-start(f32[]{:T(128)} %add.429), channel_id=1, source_target_pairs={{0,8},{1,9},{2,10},{3,11},{4,12},{5,13},{6,14},{7,15},{8,0},{9,1},... | collective-permute-start | bytes 20 | tf_op jit(solution)/shard_map/ppermute | solution.py:76
  177.5 3.8 %collective-permute-start.11 = (f32[]{:T(128)}, f32[]{:T(128)}, u32[]{:S(2)}, u32[]{:S(2)}) collective-permute-start(f32[]{:T(128)} %add.430), channel_id=1, source_target_pairs={{0,32},{16,48},{32,0},{48,16},{64,96},{80,112},{96,64},{112,80},{1... | collective-permute-start | bytes 20 | tf_op jit(solution)/shard_map/ppermute | solution.py:76
  181.9 5.3 %collective-permute-start.12 = (f32[]{:T(128)}, f32[]{:T(128)}, u32[]{:S(2)}, u32[]{:S(2)}) collective-permute-start(f32[]{:T(128)} %add.431), channel_id=1, source_target_pairs={{0,64},{16,80},{32,96},{48,112},{64,0},{80,16},{96,32},{112,48},{1... | collective-permute-start | bytes 20 | tf_op jit(solution)/shard_map/ppermute | solution.py:76
  187.7 5.3 %collective-permute-start.13 = (f32[]{:T(128)}, f32[]{:T(128)}, u32[]{:S(2)}, u32[]{:S(2)}) collective-permute-start(f32[]{:T(128)} %add.432), channel_id=1, source_target_pairs={{0,128},{16,144},{32,160},{48,176},{64,192},{80,208},{96,224},{112... | collective-permute-start | bytes 20 | tf_op jit(solution)/shard_map/ppermute | solution.py:76
  (9 other events, 19.9 us)
where the time goes:
time: 197 us; the launch traced here: 195 us
  other arithmetic  56.9 us (29%)
  local copies, waits for them, and re-layouts  49.7 us (25%)
  waiting for transfers between devices  44.3 us (22%)
  starting transfers between devices  33.9 us (17%)
  between operations  9.82 us (5%)
    ppermute x6, waiting for transfers between devices, total(): value = value + lax.ppermute(value, axis, pairs)  19.5 us
    gather x4, local copies, waits for them, and re-layouts, on_device(): innovation = inner.reshape(-1)[flat[step]] - obs_value[0, 0, step]  13.7 us
    ppermute x2, waiting for transfers between devices, grow(): lax.ppermute(lax.slice_in_dim(block, size - width, size, axis=dim), axis,...  12.5 us
    ppermute x2, starting transfers between devices, fold(): from_low = lax.ppermute(bottom, axis, down)  11.5 us
    slice x3, local copies, waits for them, and re-layouts, grow(): lax.slice_in_dim(block, size - width, size, axis=dim)  9.81 us
    ppermute x6, starting transfers between devices, total(): value = value + lax.ppermute(value, axis, pairs)  9.78 us
    add x3, other arithmetic, on_device(): adjoint = reverse_step(adjoint + injections[step])  8.95 us
    concatenate x2, other arithmetic, grow(): return jnp.concatenate([low, block, high], axis=dim)  8.85 us
  transfers between devices with their start and end apart: 14, of which 14 were waited for; matrix products, arithmetic and copies ran while one was open for 4% of the time, Pallas kernels for 0%

commit v1 on v0

--- a/solution.py
+++ b/solution.py
@@ -128,18 +128,16 @@
         return a + vertical(a, mixing) + back
 
     flat = obs_level[0, 0] * (rows * cols) + obs_cell[0, 0]
-    local_cost = jnp.zeros((), jnp.float32)
-    injections = []
+    inner = []
     for step in range(STEPS):
         state = forward_step(state)
-        inner = state[:, h : h + rows, h : h + cols]
-        innovation = inner.reshape(-1)[flat[step]] - obs_value[0, 0, step]
-        weighted = obs_weight[0, 0, step] * innovation
-        local_cost = local_cost + 0.5 * jnp.sum(weighted * innovation)
-        injections.append(weighted)
+        inner.append(state[:, h : h + rows, h : h + cols])
     block = levels * rows * cols
     spots = jnp.arange(STEPS, dtype=jnp.int32)[:, None] * block + flat
-    injected = jnp.zeros((STEPS * block,), jnp.float32).at[spots].add(jnp.stack(injections))
+    innovation = jnp.stack(inner).reshape(-1)[spots] - obs_value[0, 0]
+    weighted = obs_weight[0, 0] * innovation
+    local_cost = 0.5 * jnp.sum(weighted * innovation)
+    injected = jnp.zeros((STEPS * block,), jnp.float32).at[spots].add(weighted)
     injected = injected.reshape(STEPS, levels, rows, cols)
     injections = [jnp.pad(injected[k], ((0, 0), (h, h), (h, h))) for k in range(STEPS)]
     adjoint = jnp.zeros_like(injections[0])

time: 197 us -> 178 us (0.904)
  waiting for transfers between devices: 44.3 us -> 32.3 us
  starting transfers between devices: 33.9 us -> 41.5 us
  other arithmetic: 56.9 us -> 49.7 us
  local copies, waits for them, and re-layouts: 49.7 us -> 45.6 us
    ppermute x6, starting transfers between devices: 9.78 us -> 18.2 us  [total(): value = value + lax.ppermute(value, axis, pairs)]
    slice x1 -> x0, other arithmetic: 8.13 us -> none  [on_device(): inner = state[:, h:h + rows, h:h + cols]]
    another operation x0 -> x2, other arithmetic: none -> 6.51 us  [on_device(): innovation = jnp.stack(inner).reshape(-1)[spots] - obs_value[0, 0]]
    ppermute x2, waiting for transfers between devices: 12.5 us -> 6.47 us  [grow(): lax.ppermute(lax.slice_in_dim(block, size - width, size, axis=dim), axis,...]
    ppermute x6, waiting for transfers between devices: 19.5 us -> 14.7 us  [total(): value = value + lax.ppermute(value, axis, pairs)]
    unnamed x6 -> x5, other arithmetic: 4.2 us -> 1.78 us
    slice x4 -> x0, local copies, waits for them, and re-layouts: 2 us -> none  [the longest x2 1.98 us: on_device(): inner = state[:, h:h + rows, h:h + cols]]
    ppermute x2, starting transfers between devices: 5.29 us -> 7.26 us  [grow(): high = lax.ppermute(lax.slice_in_dim(block, 0, width, axis=dim), axis, down)]
  transfers between devices with their start and end apart: 14 -> 14, of which waited for: 14 -> 12; matrix products, arithmetic and copies ran while one was open for 4% -> 6% of each run, Pallas kernels for 0% -> 0%
where the time goes in v1:
time: 178 us; the launch traced here: 177 us
  other arithmetic  49.7 us (28%)
  local copies, waits for them, and re-layouts  45.6 us (26%)
  starting transfers between devices  41.5 us (23%)
  waiting for transfers between devices  32.3 us (18%)
  between operations  8.22 us (5%)
    ppermute x6, starting transfers between devices, total(): value = value + lax.ppermute(value, axis, pairs)  18.2 us
    ppermute x6, waiting for transfers between devices, total(): value = value + lax.ppermute(value, axis, pairs)  14.7 us
    gather x2, local copies, waits for them, and re-layouts, on_device(): innovation = jnp.stack(inner).reshape(-1)[spots] - obs_value[0, 0]  12.5 us
    ppermute x2, starting transfers between devices, fold(): from_low = lax.ppermute(bottom, axis, down)  9.84 us
    add x3, other arithmetic, on_device(): adjoint = reverse_step(adjoint + injections[step])  8.95 us
    concatenate x2, other arithmetic, grow(): return jnp.concatenate([low, block, high], axis=dim)  8.65 us
    sub x3, other arithmetic, forward_step(): return x + vertical(x, mixing) - flow  8.2 us
    slice x3, local copies, waits for them, and re-layouts, grow(): lax.slice_in_dim(block, size - width, size, axis=dim)  8.06 us
  transfers between devices with their start and end apart: 14, of which 12 were waited for; matrix products, arithmetic and copies ran while one was open for 6% of the time, Pallas kernels for 0%

profile of v1, /device:TPU:6, one launch (start us, length us, event | category | flops | bytes accessed | tf_op | source)
XLA Modules:
  0.0 177.3 jit_solution(17496793594873422259)
XLA Ops:
  5.9 7.3 %collective-permute-start.1 = (f32[5,64,4,128]{3,2,1,0:T(4,128)S(1)}, f32[5,64,4,128]{3,2,1,0:T(4,128)S(1)}, u32[]{:S(2)}, u32[]{:S(2)}) collective-permute-start(f32[5,64,4,128]{3,2,1,0:T(4,128)S(1)} %get-tuple-element.18), channel_id=1, source_target_pairs={{16,0},{32,16},{48,32},{64,48},{80,64},{96,80},{112,96},{128,112},... | collective-permute-start | bytes 1966088 | tf_op jit(solution)/shard_map/ppermute | solution.py:44
  13.3 6.2 %collective-permute-done = f32[5,64,4,128]{3,2,1,0:T(4,128)S(1)} collective-permute-done((f32[5,64,4,128]{3,2,1,0:T(4,128)S(1)}, f32[5,64,4,128]{3,2,1,0:T(4,128)S(1)}, u32[]{:S(2)}, u32[]{:S(2)}) %collective-permute-start) | collective-permute-done | bytes 655392 | tf_op jit(solution)/shard_map/ppermute | solution.py:43
  22.7 4.4 %fusion.63 = (f32[5,64,24,4]{3,2,1,0:T(8,128)}, f32[5,64,24,4]{3,2,1,0:T(8,128)}) fusion(f32[5,64,24,128]{3,2,1,0:T(8,128)S(1)} %pad_maximum_fusion.1), kind=kLoop, calls=%fused_computation.137 | loop fusion | bytes 491520 | tf_op jit(solution)/shard_map/slice | solution.py:43
  27.2 3.4 %copy.24 = f32[5,64,24,4]{1,2,3,0:T(8,128)S(1)} copy(f32[5,64,24,4]{3,2,1,0:T(8,128)} %get-tuple-element.15) | data formatting | bytes 245760 | tf_op jit(solution)/shard_map/slice | solution.py:43
  32.8 3.9 %copy.25 = f32[5,64,24,4]{1,2,3,0:T(8,128)} copy(f32[5,64,24,4]{3,2,1,0:T(8,128)} %get-tuple-element.16) | data formatting | bytes 245760 | tf_op jit(solution)/shard_map/slice | solution.py:44
  37.0 3.6 %copy.26 = f32[5,64,24,4]{3,2,1,0:T(8,128)} copy(f32[5,64,24,4]{1,2,3,0:T(8,128)} %collective-permute-done.2) | data formatting | bytes 245760 | tf_op jit(solution)/shard_map/ppermute | solution.py:43
  40.6 4.7 %collective-permute-done.3 = f32[5,64,24,4]{1,2,3,0:T(8,128)} collective-permute-done((f32[5,64,24,4]{1,2,3,0:T(8,128)}, f32[5,64,24,4]{1,2,3,0:T(8,128)}, u32[]{:S(2)}, u32[]{:S(2)}) %collective-permute-start.3) | collective-permute-done | bytes 122912 | tf_op jit(solution)/shard_map/ppermute | solution.py:44
  45.3 3.7 %copy.27 = f32[5,64,24,4]{3,2,1,0:T(8,128)} copy(f32[5,64,24,4]{1,2,3,0:T(8,128)} %collective-permute-done.3) | data formatting | bytes 245760 | tf_op jit(solution)/shard_map/ppermute | solution.py:44
  49.0 8.1 %pad_maximum_fusion = f32[5,64,24,136]{3,2,1,0:T(8,128)S(1)} fusion(f32[5,64,24,4]{3,2,1,0:T(8,128)} %copy.27, f32[5,64,4,128]{3,2,1,0:T(4,128)} %copy-done.6, f32[5,64,16,128]{3,2,1,0:T(8,128)S(1)} %bitcast_dynamic-update-slice_fusion, f32[5,64,4,128]{3,2,1,0:T(4,128)S(1)} %collective-permute-done, f32[5,64,24,4]{3,2,1,0:T(8,128)} %copy.26), kind=kLoop, calls=%fused_computation.2 | loop fusion | flops 4177920 | bytes 8355840 | tf_op jit(solution)/shard_map/concatenate | solution.py:45
  58.0 3.7 %fusion.9 = (f32[64,24,136]{2,1,0:T(8,128)S(1)}, f32[64,24,136]{2,1,0:T(8,128)S(1)}, f32[64,24,136]{2,1,0:T(8,128)S(1)}, f32[64,24,136]{2,1,0:T(8,128)}) fusion(f32[64,24,136]{2,1,0:T(8,128)S(1)} %get-tuple-element.14, f32[63,24,136]{2,1,0:T(8,128)S(1)} %fusion.49, f32[5,64,24,136]{3,2,1,0:T(8,128)S(1)} %pad_maximum_fusion, ...), kind=kLoop, calls=%fused_computation.36 | loop fusion | flops 3133440 | bytes 11685120 | tf_op jit(solution)/shard_map/sub | solution.py:120
  70.6 3.9 %slice_bitcast_fusion.7 = (f32[1,64,16,128]{3,2,1,0:T(8,128)S(1)}, f32[1,64,16,128]{3,2,1,0:T(8,128)S(1)}) fusion(f32[64,24,136]{2,1,0:T(8,128)S(1)} %fusion.19, f32[64,24,136]{2,1,0:T(8,128)S(1)} %get-tuple-element.31, f32[64,24,136]{2,1,0:T(8,128)S(1)} %get-tuple-element.11, f32[64,24,136]{2,1,0:T(8,128)S(1)} %get-tuple-element.30, ...), kind=kLoop, calls=%fused_computation.122 | loop fusion | flops 1572864 | bytes 7113984 | tf_op jit(solution)/shard_map/stack | solution.py:137
  74.4 2.7 %pad_maximum_fusion.2 = f32[4,64,16,128]{3,2,1,0:T(8,128)} fusion(f32[1,64,16,128]{3,2,1,0:T(8,128)S(1)} %get-tuple-element.26, f32[1,64,16,128]{3,2,1,0:T(8,128)S(1)} %get-tuple-element.25, f32[1,64,16,128]{3,2,1,0:T(8,128)} %get-tuple-element.37, f32[1,64,16,128]{3,2,1,0:T(8,128)} %get-tuple-element.38), kind=kLoop, calls=%fused_computation.4 | loop fusion | flops 1572864 | bytes 4194304 | tf_op jit(solution)/shard_map/stack | solution.py:137
  77.1 12.5 %gather_fusion = f32[1024]{0:T(1024)S(1)} fusion(f32[524288]{0:T(1024)} %bitcast.108, s32[1024]{0:T(1024)S(1)} %broadcast_clamp_fusion), kind=kCustom, calls=%fused_computation | custom fusion | bytes 12288 | tf_op jit(solution)/shard_map/gather | solution.py:137
  90.3 7.3 %scatter_custom_fusion = f32[524288]{0:T(1024)} fusion(s32[1024]{0:T(1024)S(1)} %bitcast.118, f32[1024]{0:T(1024)S(1)} %bitcast.119, f32[]{:T(128)} %constant.15.clone.1), kind=kCustom, calls=%fused_computation.94 | custom fusion | flops 1024 | bytes 2097156 | tf_op jit(solution)/shard_map/scatter-add | solution.py:140
  100.7 4.1 %fusion.1 = f32[64,24,136]{2,1,0:T(8,128)S(1)} fusion(f32[64,16,128]{2,1,0:T(8,128)S(1)} %bitcast.111, f32[64,24,136]{2,1,0:T(8,128)S(1)} %pad.181, f32[64,16,128]{2,1,0:T(8,128)S(1)} %bitcast.114, f32[63,24,136]{2,1,0:T(8,128)S(1)} %fusion.41, f32[64,24,136]{2,1,0:T(8,128)S(1)} %get-tuple-element.5, f32[64,24,136]{2,1,0:T(8,128)S(1)} %get-tuple-element.10, ...), kind=kLoop, calls=%fused_computation.28 | loop fusion | flops 2924544 | bytes 7720192 | tf_op jit(solution)/shard_map/add | solution.py:145
  115.5 2.6 %collective-permute-start.5 = (f32[65,24,4]{0,1,2:T(8,128)S(1)}, f32[65,24,4]{0,1,2:T(8,128)S(1)}, u32[]{:S(2)}, u32[]{:S(2)}) collective-permute-start(f32[65,24,4]{0,1,2:T(8,128)S(1)} %concatenate.85.clone), channel_id=1, source_target_pairs={{1,0},{2,1},{3,2},{4,3},{5,4},{6,5},{7,6},{8,7},{9,8},{10,9},{11,1... | collective-permute-start | bytes 74888 | tf_op jit(solution)/shard_map/ppermute | solution.py:55
  118.1 2.6 %collective-permute-done.4 = f32[65,24,4]{0,1,2:T(8,128)S(1)} collective-permute-done((f32[65,24,4]{0,1,2:T(8,128)S(1)}, f32[65,24,4]{0,1,2:T(8,128)S(1)}, u32[]{:S(2)}, u32[]{:S(2)}) %collective-permute-start.4) | collective-permute-done | bytes 24992 | tf_op jit(solution)/shard_map/ppermute | solution.py:54
  125.8 7.3 %collective-permute-start.7 = (f32[65,4,128]{2,1,0:T(4,128)S(1)}, f32[65,4,128]{2,1,0:T(4,128)S(1)}, u32[]{:S(2)}, u32[]{:S(2)}) collective-permute-start(f32[65,4,128]{2,1,0:T(4,128)S(1)} %concatenate.87), channel_id=1, source_target_pairs={{16,0},{32,16},{48,32},{64,48},{80,64},{96,80},{112,96},{128,112},... | collective-permute-start | bytes 399368 | tf_op jit(solution)/shard_map/ppermute | solution.py:55
  137.4 2.9 %collective-permute-start.8 = (f32[]{:T(128)}, f32[]{:T(128)}, u32[]{:S(2)}, u32[]{:S(2)}) collective-permute-start(f32[]{:T(128)} %add.364), channel_id=1, source_target_pairs={{0,2},{1,3},{2,0},{3,1},{4,6},{5,7},{6,4},{7,5},{8,10},{9,11},{10,... | collective-permute-start | bytes 20 | tf_op jit(solution)/shard_map/ppermute | solution.py:76
  143.1 8.4 %collective-permute-start.9 = (f32[]{:T(128)}, f32[]{:T(128)}, u32[]{:S(2)}, u32[]{:S(2)}) collective-permute-start(f32[]{:T(128)} %add.365), channel_id=1, source_target_pairs={{0,4},{1,5},{2,6},{3,7},{4,0},{5,1},{6,2},{7,3},{8,12},{9,13},{10,... | collective-permute-start | bytes 20 | tf_op jit(solution)/shard_map/ppermute | solution.py:76
  152.3 2.7 %collective-permute-start.10 = (f32[]{:T(128)}, f32[]{:T(128)}, u32[]{:S(2)}, u32[]{:S(2)}) collective-permute-start(f32[]{:T(128)} %add.366), channel_id=1, source_target_pairs={{0,8},{1,9},{2,10},{3,11},{4,12},{5,13},{6,14},{7,15},{8,0},{9,1},... | collective-permute-start | bytes 20 | tf_op jit(solution)/shard_map/ppermute | solution.py:76
  155.0 4.8 %collective-permute-done.10 = f32[]{:T(128)} collective-permute-done((f32[]{:T(128)}, f32[]{:T(128)}, u32[]{:S(2)}, u32[]{:S(2)}) %collective-permute-start.10) | collective-permute-done | bytes 36 | tf_op jit(solution)/shard_map/ppermute | solution.py:76
  166.0 3.7 %collective-permute-done.12 = f32[]{:T(128)} collective-permute-done((f32[]{:T(128)}, f32[]{:T(128)}, u32[]{:S(2)}, u32[]{:S(2)}) %collective-permute-start.12) | collective-permute-done | bytes 36 | tf_op jit(solution)/shard_map/ppermute | solution.py:76
  171.8 3.7 %collective-permute-done.13 = f32[]{:T(128)} collective-permute-done((f32[]{:T(128)}, f32[]{:T(128)}, u32[]{:S(2)}, u32[]{:S(2)}) %collective-permute-start.13) | collective-permute-done | bytes 36 | tf_op jit(solution)/shard_map/ppermute | solution.py:76
  (108 shorter events, 50.9 us)
Async XLA Ops:
  0.6 2.6 %copy-start.7 = (f32[64,16,128]{2,1,0:T(8,128)S(1)}, f32[64,16,128]{2,1,0:T(8,128)}, u32[]{:S(2)}) copy-start(f32[64,16,128]{2,1,0:T(8,128)} %param.11) | copy-start | bytes 1572868
  3.7 9.5 %copy-start.11 = (s32[1,1,4,256]{3,2,1,0:T(4,128)S(1)}, s32[1,1,4,256]{3,2,1,0:T(4,128)}, u32[]{:S(2)}) copy-start(s32[1,1,4,256]{3,2,1,0:T(4,128)} %param.16) | copy-start | bytes 12292
  3.7 9.5 %copy-start.12 = (s32[1,1,4,256]{3,2,1,0:T(4,128)S(1)}, s32[1,1,4,256]{3,2,1,0:T(4,128)}, u32[]{:S(2)}) copy-start(s32[1,1,4,256]{3,2,1,0:T(4,128)} %param.17) | copy-start | bytes 12292
  4.0 15.5 %collective-permute-start = (f32[5,64,4,128]{3,2,1,0:T(4,128)S(1)}, f32[5,64,4,128]{3,2,1,0:T(4,128)S(1)}, u32[]{:S(2)}, u32[]{:S(2)}) collective-permute-start(f32[5,64,4,128]{3,2,1,0:T(4,128)S(1)} %get-tuple-element.17), channel_id=1, source_target_pairs={{0,16},{16,32},{32,48},{48,64},{64,80},{80,96},{96,112},{112,128},... | collective-permute-start | bytes 1966088 | tf_op jit(solution)/shard_map/ppermute | solution.py:43
  5.9 15.3 %collective-permute-start.1 = (f32[5,64,4,128]{3,2,1,0:T(4,128)S(1)}, f32[5,64,4,128]{3,2,1,0:T(4,128)S(1)}, u32[]{:S(2)}, u32[]{:S(2)}) collective-permute-start(f32[5,64,4,128]{3,2,1,0:T(4,128)S(1)} %get-tuple-element.18), channel_id=1, source_target_pairs={{16,0},{32,16},{48,32},{64,48},{80,64},{96,80},{112,96},{128,112},... | collective-permute-start | bytes 1966088 | tf_op jit(solution)/shard_map/ppermute | solution.py:44
  30.5 6.4 %collective-permute-start.2 = (f32[5,64,24,4]{1,2,3,0:T(8,128)S(1)}, f32[5,64,24,4]{1,2,3,0:T(8,128)}, u32[]{:S(2)}, u32[]{:S(2)}) collective-permute-start(f32[5,64,24,4]{1,2,3,0:T(8,128)S(1)} %copy.24), channel_id=1, source_target_pairs={{0,1},{1,2},{2,3},{3,4},{4,5},{5,6},{6,7},{7,8},{8,9},{9,10},{10,1... | collective-permute-start | bytes 368648 | tf_op jit(solution)/shard_map/ppermute | solution.py:43
  36.7 8.6 %collective-permute-start.3 = (f32[5,64,24,4]{1,2,3,0:T(8,128)}, f32[5,64,24,4]{1,2,3,0:T(8,128)}, u32[]{:S(2)}, u32[]{:S(2)}) collective-permute-start(f32[5,64,24,4]{1,2,3,0:T(8,128)} %copy.25), channel_id=1, source_target_pairs={{1,0},{2,1},{3,2},{4,3},{5,4},{6,5},{7,6},{8,7},{9,8},{10,9},{11,1... | collective-permute-start | bytes 368648 | tf_op jit(solution)/shard_map/ppermute | solution.py:44
  57.1 8.7 %copy-start = (f32[5,64,24,136]{3,2,1,0:T(8,128)}, f32[5,64,24,136]{3,2,1,0:T(8,128)S(1)}, u32[]{:S(2)}) copy-start(f32[5,64,24,136]{3,2,1,0:T(8,128)S(1)} %pad_maximum_fusion) | copy-start | bytes 12533764
  57.8 12.8 %copy-start.1 = (f32[64,24,136]{2,1,0:T(8,128)}, f32[64,24,136]{2,1,0:T(8,128)S(1)}, u32[]{:S(2)}) copy-start(f32[64,24,136]{2,1,0:T(8,128)S(1)} %get-tuple-element.11) | copy-start | bytes 2506756
  77.1 12.5 %copy-start.13 = (f32[1,1,4,256]{3,2,1,0:T(4,128)S(1)}, f32[1,1,4,256]{3,2,1,0:T(4,128)}, u32[]{:S(2)}) copy-start(f32[1,1,4,256]{3,2,1,0:T(4,128)} %param.19) | copy-start | bytes 12292
  77.1 12.6 %copy-start.14 = (f32[1,1,4,256]{3,2,1,0:T(4,128)S(1)}, f32[1,1,4,256]{3,2,1,0:T(4,128)}, u32[]{:S(2)}) copy-start(f32[1,1,4,256]{3,2,1,0:T(4,128)} %param.18) | copy-start | bytes 12292
  100.7 4.4 %slice-start = ((s8[7864320]{0:T(1024)(128)(4,1)}), s8[4194304]{0:T(1024)(128)(4,1)S(1)}, s32[]{:S(2)}) async-start(s8[7864320]{0:T(1024)(128)(4,1)} %bitcast.106), calls=%async_computation | async-start | bytes 8388608
  100.7 4.4 %slice-start.1 = ((s8[7864320]{0:T(1024)(128)(4,1)}), s8[3670016]{0:T(1024)(128)(4,1)S(1)}, s32[]{:S(2)}) async-start(s8[7864320]{0:T(1024)(128)(4,1)} %bitcast.106), calls=%async_computation.1 | async-start | bytes 7340032
  114.3 8.1 %copy-start.4 = (f32[64,24,136]{2,1,0:T(8,128)S(1)}, f32[64,24,136]{2,1,0:T(8,128)}, u32[]{:S(2)}) copy-start(f32[64,24,136]{2,1,0:T(8,128)} %copy-done.3) | copy-start | bytes 2506756
  115.1 5.6 %collective-permute-start.4 = (f32[65,24,4]{0,1,2:T(8,128)S(1)}, f32[65,24,4]{0,1,2:T(8,128)S(1)}, u32[]{:S(2)}, u32[]{:S(2)}) collective-permute-start(f32[65,24,4]{0,1,2:T(8,128)S(1)} %concatenate.84.clone), channel_id=1, source_target_pairs={{0,1},{1,2},{2,3},{3,4},{4,5},{5,6},{6,7},{7,8},{8,9},{9,10},{10,1... | collective-permute-start | bytes 74888 | tf_op jit(solution)/shard_map/ppermute | solution.py:54
  115.5 5.7 %collective-permute-start.5 = (f32[65,24,4]{0,1,2:T(8,128)S(1)}, f32[65,24,4]{0,1,2:T(8,128)S(1)}, u32[]{:S(2)}, u32[]{:S(2)}) collective-permute-start(f32[65,24,4]{0,1,2:T(8,128)S(1)} %concatenate.85.clone), channel_id=1, source_target_pairs={{1,0},{2,1},{3,2},{4,3},{5,4},{6,5},{7,6},{8,7},{9,8},{10,9},{11,1... | collective-permute-start | bytes 74888 | tf_op jit(solution)/shard_map/ppermute | solution.py:55
  123.9 9.9 %collective-permute-start.6 = (f32[65,4,128]{2,1,0:T(4,128)S(1)}, f32[65,4,128]{2,1,0:T(4,128)S(1)}, u32[]{:S(2)}, u32[]{:S(2)}) collective-permute-start(f32[65,4,128]{2,1,0:T(4,128)S(1)} %concatenate.86), channel_id=1, source_target_pairs={{0,16},{16,32},{32,48},{48,64},{64,80},{80,96},{96,112},{112,128},... | collective-permute-start | bytes 399368 | tf_op jit(solution)/shard_map/ppermute | solution.py:54
  125.8 9.8 %collective-permute-start.7 = (f32[65,4,128]{2,1,0:T(4,128)S(1)}, f32[65,4,128]{2,1,0:T(4,128)S(1)}, u32[]{:S(2)}, u32[]{:S(2)}) collective-permute-start(f32[65,4,128]{2,1,0:T(4,128)S(1)} %concatenate.87), channel_id=1, source_target_pairs={{16,0},{32,16},{48,32},{64,48},{80,64},{96,80},{112,96},{128,112},... | collective-permute-start | bytes 399368 | tf_op jit(solution)/shard_map/ppermute | solution.py:55
  137.4 5.0 %collective-permute-start.8 = (f32[]{:T(128)}, f32[]{:T(128)}, u32[]{:S(2)}, u32[]{:S(2)}) collective-permute-start(f32[]{:T(128)} %add.364), channel_id=1, source_target_pairs={{0,2},{1,3},{2,0},{3,1},{4,6},{5,7},{6,4},{7,5},{8,10},{9,11},{10,... | collective-permute-start | bytes 20 | tf_op jit(solution)/shard_map/ppermute | solution.py:76
  143.1 8.6 %collective-permute-start.9 = (f32[]{:T(128)}, f32[]{:T(128)}, u32[]{:S(2)}, u32[]{:S(2)}) collective-permute-start(f32[]{:T(128)} %add.365), channel_id=1, source_target_pairs={{0,4},{1,5},{2,6},{3,7},{4,0},{5,1},{6,2},{7,3},{8,12},{9,13},{10,... | collective-permute-start | bytes 20 | tf_op jit(solution)/shard_map/ppermute | solution.py:76
  152.3 7.5 %collective-permute-start.10 = (f32[]{:T(128)}, f32[]{:T(128)}, u32[]{:S(2)}, u32[]{:S(2)}) collective-permute-start(f32[]{:T(128)} %add.366), channel_id=1, source_target_pairs={{0,8},{1,9},{2,10},{3,11},{4,12},{5,13},{6,14},{7,15},{8,0},{9,1},... | collective-permute-start | bytes 20 | tf_op jit(solution)/shard_map/ppermute | solution.py:76
  160.4 3.6 %collective-permute-start.11 = (f32[]{:T(128)}, f32[]{:T(128)}, u32[]{:S(2)}, u32[]{:S(2)}) collective-permute-start(f32[]{:T(128)} %add.367), channel_id=1, source_target_pairs={{0,32},{16,48},{32,0},{48,16},{64,96},{80,112},{96,64},{112,80},{1... | collective-permute-start | bytes 20 | tf_op jit(solution)/shard_map/ppermute | solution.py:76
  164.7 5.1 %collective-permute-start.12 = (f32[]{:T(128)}, f32[]{:T(128)}, u32[]{:S(2)}, u32[]{:S(2)}) collective-permute-start(f32[]{:T(128)} %add.368), channel_id=1, source_target_pairs={{0,64},{16,80},{32,96},{48,112},{64,0},{80,16},{96,32},{112,48},{1... | collective-permute-start | bytes 20 | tf_op jit(solution)/shard_map/ppermute | solution.py:76
  170.4 5.1 %collective-permute-start.13 = (f32[]{:T(128)}, f32[]{:T(128)}, u32[]{:S(2)}, u32[]{:S(2)}) collective-permute-start(f32[]{:T(128)} %add.369), channel_id=1, source_target_pairs={{0,128},{16,144},{32,160},{48,176},{64,192},{80,208},{96,224},{112... | collective-permute-start | bytes 20 | tf_op jit(solution)/shard_map/ppermute | solution.py:76
  (7 other events, 8.2 us)

commit v2 on v1

--- a/solution.py
+++ b/solution.py
@@ -139,7 +139,8 @@
     local_cost = 0.5 * jnp.sum(weighted * innovation)
     injected = jnp.zeros((STEPS * block,), jnp.float32).at[spots].add(weighted)
     injected = injected.reshape(STEPS, levels, rows, cols)
-    injections = [jnp.pad(injected[k], ((0, 0), (h, h), (h, h))) for k in range(STEPS)]
+    padded = jnp.pad(injected, ((0, 0), (0, 0), (h, h), (h, h)))
+    injections = [padded[k] for k in range(STEPS)]
     adjoint = jnp.zeros_like(injections[0])
     for step in range(STEPS - 1, -1, -1):
         adjoint = reverse_step(adjoint + injections[step])

time: 178 us -> 178 us (level)
    unnamed x41 -> x43, local copies, waits for them, and re-layouts: 5.29 us -> 5.37 us
where the time goes in v2:
time: 178 us; the launch traced here: 177 us
  other arithmetic  49.6 us (28%)
  local copies, waits for them, and re-layouts  45.2 us (25%)
  starting transfers between devices  41.5 us (23%)
  waiting for transfers between devices  32.2 us (18%)
  between operations  8.2 us (5%)
    ppermute x6, starting transfers between devices, total(): value = value + lax.ppermute(value, axis, pairs)  18.2 us
    ppermute x6, waiting for transfers between devices, total(): value = value + lax.ppermute(value, axis, pairs)  14.6 us
    gather x2, local copies, waits for them, and re-layouts, on_device(): innovation = jnp.stack(inner).reshape(-1)[spots] - obs_value[0, 0]  12.5 us
    ppermute x2, starting transfers between devices, fold(): from_low = lax.ppermute(bottom, axis, down)  9.74 us
    add x3, other arithmetic, on_device(): adjoint = reverse_step(adjoint + injections[step])  8.94 us
    concatenate x2, other arithmetic, grow(): return jnp.concatenate([low, block, high], axis=dim)  8.65 us
    sub x3, other arithmetic, forward_step(): return x + vertical(x, mixing) - flow  8.2 us
    slice x3, local copies, waits for them, and re-layouts, grow(): lax.slice_in_dim(block, size - width, size, axis=dim)  8.06 us
  transfers between devices with their start and end apart: 14, of which 12 were waited for; matrix products, arithmetic and copies ran while one was open for 6% of the time, Pallas kernels for 0%

profile of v2, /device:TPU:6, one launch (start us, length us, event | category | flops | bytes accessed | tf_op | source)
XLA Modules:
  0.0 176.6 jit_solution(17903372801443435428)
XLA Ops:
  5.9 7.3 %collective-permute-start.1 = (f32[5,64,4,128]{3,2,1,0:T(4,128)S(1)}, f32[5,64,4,128]{3,2,1,0:T(4,128)S(1)}, u32[]{:S(2)}, u32[]{:S(2)}) collective-permute-start(f32[5,64,4,128]{3,2,1,0:T(4,128)S(1)} %get-tuple-element.18), channel_id=1, source_target_pairs={{16,0},{32,16},{48,32},{64,48},{80,64},{96,80},{112,96},{128,112},... | collective-permute-start | bytes 1966088 | tf_op jit(solution)/shard_map/ppermute | solution.py:44
  13.3 6.2 %collective-permute-done = f32[5,64,4,128]{3,2,1,0:T(4,128)S(1)} collective-permute-done((f32[5,64,4,128]{3,2,1,0:T(4,128)S(1)}, f32[5,64,4,128]{3,2,1,0:T(4,128)S(1)}, u32[]{:S(2)}, u32[]{:S(2)}) %collective-permute-start) | collective-permute-done | bytes 655392 | tf_op jit(solution)/shard_map/ppermute | solution.py:43
  22.7 4.4 %fusion.66 = (f32[5,64,24,4]{3,2,1,0:T(8,128)}, f32[5,64,24,4]{3,2,1,0:T(8,128)}) fusion(f32[5,64,24,128]{3,2,1,0:T(8,128)S(1)} %pad_maximum_fusion.1), kind=kLoop, calls=%fused_computation.142 | loop fusion | bytes 491520 | tf_op jit(solution)/shard_map/slice | solution.py:43
  27.2 3.4 %copy.24 = f32[5,64,24,4]{1,2,3,0:T(8,128)S(1)} copy(f32[5,64,24,4]{3,2,1,0:T(8,128)} %get-tuple-element.15) | data formatting | bytes 245760 | tf_op jit(solution)/shard_map/slice | solution.py:43
  32.8 3.9 %copy.25 = f32[5,64,24,4]{1,2,3,0:T(8,128)} copy(f32[5,64,24,4]{3,2,1,0:T(8,128)} %get-tuple-element.16) | data formatting | bytes 245760 | tf_op jit(solution)/shard_map/slice | solution.py:44
  37.0 3.6 %copy.26 = f32[5,64,24,4]{3,2,1,0:T(8,128)} copy(f32[5,64,24,4]{1,2,3,0:T(8,128)} %collective-permute-done.2) | data formatting | bytes 245760 | tf_op jit(solution)/shard_map/ppermute | solution.py:43
  40.6 4.7 %collective-permute-done.3 = f32[5,64,24,4]{1,2,3,0:T(8,128)} collective-permute-done((f32[5,64,24,4]{1,2,3,0:T(8,128)}, f32[5,64,24,4]{1,2,3,0:T(8,128)}, u32[]{:S(2)}, u32[]{:S(2)}) %collective-permute-start.3) | collective-permute-done | bytes 122912 | tf_op jit(solution)/shard_map/ppermute | solution.py:44
  45.3 3.7 %copy.27 = f32[5,64,24,4]{3,2,1,0:T(8,128)} copy(f32[5,64,24,4]{1,2,3,0:T(8,128)} %collective-permute-done.3) | data formatting | bytes 245760 | tf_op jit(solution)/shard_map/ppermute | solution.py:44
  49.0 8.1 %pad_maximum_fusion = f32[5,64,24,136]{3,2,1,0:T(8,128)S(1)} fusion(f32[5,64,24,4]{3,2,1,0:T(8,128)} %copy.27, f32[5,64,4,128]{3,2,1,0:T(4,128)} %copy-done.7, f32[5,64,16,128]{3,2,1,0:T(8,128)S(1)} %bitcast_dynamic-update-slice_fusion, f32[5,64,4,128]{3,2,1,0:T(4,128)S(1)} %collective-permute-done, f32[5,64,24,4]{3,2,1,0:T(8,128)} %copy.26), kind=kLoop, calls=%fused_computation.8 | loop fusion | flops 4177920 | bytes 8355840 | tf_op jit(solution)/shard_map/concatenate | solution.py:45
  58.0 3.7 %fusion.3 = (f32[64,24,136]{2,1,0:T(8,128)S(1)}, f32[64,24,136]{2,1,0:T(8,128)S(1)}, f32[64,24,136]{2,1,0:T(8,128)S(1)}, f32[64,24,136]{2,1,0:T(8,128)}) fusion(f32[64,24,136]{2,1,0:T(8,128)S(1)} %get-tuple-element.14, f32[63,24,136]{2,1,0:T(8,128)S(1)} %fusion.52, f32[5,64,24,136]{3,2,1,0:T(8,128)S(1)} %pad_maximum_fusion, ...), kind=kLoop, calls=%fused_computation.32 | loop fusion | flops 3133440 | bytes 11685120 | tf_op jit(solution)/shard_map/sub | solution.py:120
  70.6 3.9 %slice_bitcast_fusion.7 = (f32[1,64,16,128]{3,2,1,0:T(8,128)S(1)}, f32[1,64,16,128]{3,2,1,0:T(8,128)S(1)}) fusion(f32[64,24,136]{2,1,0:T(8,128)S(1)} %fusion.13, f32[64,24,136]{2,1,0:T(8,128)S(1)} %get-tuple-element.27, f32[64,24,136]{2,1,0:T(8,128)S(1)} %get-tuple-element.11, f32[64,24,136]{2,1,0:T(8,128)S(1)} %get-tuple-element.26, ...), kind=kLoop, calls=%fused_computation.127 | loop fusion | flops 1572864 | bytes 7113984 | tf_op jit(solution)/shard_map/stack | solution.py:137
  74.4 2.7 %pad_maximum_fusion.2 = f32[4,64,16,128]{3,2,1,0:T(8,128)} fusion(f32[1,64,16,128]{3,2,1,0:T(8,128)S(1)} %get-tuple-element.22, f32[1,64,16,128]{3,2,1,0:T(8,128)S(1)} %get-tuple-element.21, f32[1,64,16,128]{3,2,1,0:T(8,128)} %get-tuple-element.33, f32[1,64,16,128]{3,2,1,0:T(8,128)} %get-tuple-element.34), kind=kLoop, calls=%fused_computation.10 | loop fusion | flops 1572864 | bytes 4194304 | tf_op jit(solution)/shard_map/stack | solution.py:137
  77.1 12.5 %gather_fusion = f32[1024]{0:T(1024)S(1)} fusion(f32[524288]{0:T(1024)} %bitcast.128, s32[1024]{0:T(1024)S(1)} %broadcast_clamp_fusion), kind=kCustom, calls=%fused_computation | custom fusion | bytes 12288 | tf_op jit(solution)/shard_map/gather | solution.py:137
  90.2 7.3 %scatter_custom_fusion = f32[524288]{0:T(1024)} fusion(s32[1024]{0:T(1024)S(1)} %bitcast.132, f32[1024]{0:T(1024)S(1)} %bitcast.133, f32[]{:T(128)} %constant.15.clone.1), kind=kCustom, calls=%fused_computation.99 | custom fusion | flops 1024 | bytes 2097156 | tf_op jit(solution)/shard_map/scatter-add | solution.py:140
  100.3 4.0 %fusion.19 = f32[64,24,136]{2,1,0:T(8,128)S(1)} fusion(f32[64,24,136]{2,1,0:T(8,128)S(1)} %fusion.38, f32[4,64,16,128]{3,2,1,0:T(8,128)S(1)} %bitcast.125, f32[63,24,136]{2,1,0:T(8,128)S(1)} %fusion.44, f32[64,24,136]{2,1,0:T(8,128)S(1)} %get-tuple-element.5, f32[64,24,136]{2,1,0:T(8,128)S(1)} %get-tuple-element.10, f32[64,24,136]{2,1,0:T(8,128)S(1)} %copy-done.3, ...), kind=kLoop, calls=%fused_computation.48 | loop fusion | flops 2924544 | bytes 8768768 | tf_op jit(solution)/shard_map/add | solution.py:146
  115.0 2.5 %collective-permute-start.5 = (f32[65,24,4]{0,1,2:T(8,128)S(1)}, f32[65,24,4]{0,1,2:T(8,128)S(1)}, u32[]{:S(2)}, u32[]{:S(2)}) collective-permute-start(f32[65,24,4]{0,1,2:T(8,128)S(1)} %concatenate.85.clone), channel_id=1, source_target_pairs={{1,0},{2,1},{3,2},{4,3},{5,4},{6,5},{7,6},{8,7},{9,8},{10,9},{11,1... | collective-permute-start | bytes 74888 | tf_op jit(solution)/shard_map/ppermute | solution.py:55
  117.5 2.7 %collective-permute-done.4 = f32[65,24,4]{0,1,2:T(8,128)S(1)} collective-permute-done((f32[65,24,4]{0,1,2:T(8,128)S(1)}, f32[65,24,4]{0,1,2:T(8,128)S(1)}, u32[]{:S(2)}, u32[]{:S(2)}) %collective-permute-start.4) | collective-permute-done | bytes 24992 | tf_op jit(solution)/shard_map/ppermute | solution.py:54
  125.3 7.3 %collective-permute-start.7 = (f32[65,4,128]{2,1,0:T(4,128)S(1)}, f32[65,4,128]{2,1,0:T(4,128)S(1)}, u32[]{:S(2)}, u32[]{:S(2)}) collective-permute-start(f32[65,4,128]{2,1,0:T(4,128)S(1)} %concatenate.87), channel_id=1, source_target_pairs={{16,0},{32,16},{48,32},{64,48},{80,64},{96,80},{112,96},{128,112},... | collective-permute-start | bytes 399368 | tf_op jit(solution)/shard_map/ppermute | solution.py:55
  136.9 3.0 %collective-permute-start.8 = (f32[]{:T(128)}, f32[]{:T(128)}, u32[]{:S(2)}, u32[]{:S(2)}) collective-permute-start(f32[]{:T(128)} %add.358), channel_id=1, source_target_pairs={{0,2},{1,3},{2,0},{3,1},{4,6},{5,7},{6,4},{7,5},{8,10},{9,11},{10,... | collective-permute-start | bytes 20 | tf_op jit(solution)/shard_map/ppermute | solution.py:76
  142.6 8.3 %collective-permute-start.9 = (f32[]{:T(128)}, f32[]{:T(128)}, u32[]{:S(2)}, u32[]{:S(2)}) collective-permute-start(f32[]{:T(128)} %add.359), channel_id=1, source_target_pairs={{0,4},{1,5},{2,6},{3,7},{4,0},{5,1},{6,2},{7,3},{8,12},{9,13},{10,... | collective-permute-start | bytes 20 | tf_op jit(solution)/shard_map/ppermute | solution.py:76
  151.7 2.8 %collective-permute-start.10 = (f32[]{:T(128)}, f32[]{:T(128)}, u32[]{:S(2)}, u32[]{:S(2)}) collective-permute-start(f32[]{:T(128)} %add.360), channel_id=1, source_target_pairs={{0,8},{1,9},{2,10},{3,11},{4,12},{5,13},{6,14},{7,15},{8,0},{9,1},... | collective-permute-start | bytes 20 | tf_op jit(solution)/shard_map/ppermute | solution.py:76
  154.5 4.7 %collective-permute-done.10 = f32[]{:T(128)} collective-permute-done((f32[]{:T(128)}, f32[]{:T(128)}, u32[]{:S(2)}, u32[]{:S(2)}) %collective-permute-start.10) | collective-permute-done | bytes 36 | tf_op jit(solution)/shard_map/ppermute | solution.py:76
  165.4 3.7 %collective-permute-done.12 = f32[]{:T(128)} collective-permute-done((f32[]{:T(128)}, f32[]{:T(128)}, u32[]{:S(2)}, u32[]{:S(2)}) %collective-permute-start.12) | collective-permute-done | bytes 36 | tf_op jit(solution)/shard_map/ppermute | solution.py:76
  171.2 3.7 %collective-permute-done.13 = f32[]{:T(128)} collective-permute-done((f32[]{:T(128)}, f32[]{:T(128)}, u32[]{:S(2)}, u32[]{:S(2)}) %collective-permute-start.13) | collective-permute-done | bytes 36 | tf_op jit(solution)/shard_map/ppermute | solution.py:76
  (109 shorter events, 50.5 us)
Async XLA Ops:
  3.7 9.5 %copy-start.12 = (s32[1,1,4,256]{3,2,1,0:T(4,128)S(1)}, s32[1,1,4,256]{3,2,1,0:T(4,128)}, u32[]{:S(2)}) copy-start(s32[1,1,4,256]{3,2,1,0:T(4,128)} %param.16) | copy-start | bytes 12292
  3.7 9.5 %copy-start.13 = (s32[1,1,4,256]{3,2,1,0:T(4,128)S(1)}, s32[1,1,4,256]{3,2,1,0:T(4,128)}, u32[]{:S(2)}) copy-start(s32[1,1,4,256]{3,2,1,0:T(4,128)} %param.17) | copy-start | bytes 12292
  4.0 15.5 %collective-permute-start = (f32[5,64,4,128]{3,2,1,0:T(4,128)S(1)}, f32[5,64,4,128]{3,2,1,0:T(4,128)S(1)}, u32[]{:S(2)}, u32[]{:S(2)}) collective-permute-start(f32[5,64,4,128]{3,2,1,0:T(4,128)S(1)} %get-tuple-element.17), channel_id=1, source_target_pairs={{0,16},{16,32},{32,48},{48,64},{64,80},{80,96},{96,112},{112,128},... | collective-permute-start | bytes 1966088 | tf_op jit(solution)/shard_map/ppermute | solution.py:43
  5.9 15.3 %collective-permute-start.1 = (f32[5,64,4,128]{3,2,1,0:T(4,128)S(1)}, f32[5,64,4,128]{3,2,1,0:T(4,128)S(1)}, u32[]{:S(2)}, u32[]{:S(2)}) collective-permute-start(f32[5,64,4,128]{3,2,1,0:T(4,128)S(1)} %get-tuple-element.18), channel_id=1, source_target_pairs={{16,0},{32,16},{48,32},{64,48},{80,64},{96,80},{112,96},{128,112},... | collective-permute-start | bytes 1966088 | tf_op jit(solution)/shard_map/ppermute | solution.py:44
  30.5 6.4 %collective-permute-start.2 = (f32[5,64,24,4]{1,2,3,0:T(8,128)S(1)}, f32[5,64,24,4]{1,2,3,0:T(8,128)}, u32[]{:S(2)}, u32[]{:S(2)}) collective-permute-start(f32[5,64,24,4]{1,2,3,0:T(8,128)S(1)} %copy.24), channel_id=1, source_target_pairs={{0,1},{1,2},{2,3},{3,4},{4,5},{5,6},{6,7},{7,8},{8,9},{9,10},{10,1... | collective-permute-start | bytes 368648 | tf_op jit(solution)/shard_map/ppermute | solution.py:43
  36.7 8.6 %collective-permute-start.3 = (f32[5,64,24,4]{1,2,3,0:T(8,128)}, f32[5,64,24,4]{1,2,3,0:T(8,128)}, u32[]{:S(2)}, u32[]{:S(2)}) collective-permute-start(f32[5,64,24,4]{1,2,3,0:T(8,128)} %copy.25), channel_id=1, source_target_pairs={{1,0},{2,1},{3,2},{4,3},{5,4},{6,5},{7,6},{8,7},{9,8},{10,9},{11,1... | collective-permute-start | bytes 368648 | tf_op jit(solution)/shard_map/ppermute | solution.py:44
  57.1 8.7 %copy-start = (f32[5,64,24,136]{3,2,1,0:T(8,128)}, f32[5,64,24,136]{3,2,1,0:T(8,128)S(1)}, u32[]{:S(2)}) copy-start(f32[5,64,24,136]{3,2,1,0:T(8,128)S(1)} %pad_maximum_fusion) | copy-start | bytes 12533764
  57.8 12.8 %copy-start.2 = (f32[64,24,136]{2,1,0:T(8,128)}, f32[64,24,136]{2,1,0:T(8,128)S(1)}, u32[]{:S(2)}) copy-start(f32[64,24,136]{2,1,0:T(8,128)S(1)} %get-tuple-element.11) | copy-start | bytes 2506756
  77.1 12.5 %copy-start.14 = (f32[1,1,4,256]{3,2,1,0:T(4,128)S(1)}, f32[1,1,4,256]{3,2,1,0:T(4,128)}, u32[]{:S(2)}) copy-start(f32[1,1,4,256]{3,2,1,0:T(4,128)} %param.19) | copy-start | bytes 12292
  77.1 12.5 %copy-start.15 = (f32[1,1,4,256]{3,2,1,0:T(4,128)S(1)}, f32[1,1,4,256]{3,2,1,0:T(4,128)}, u32[]{:S(2)}) copy-start(f32[1,1,4,256]{3,2,1,0:T(4,128)} %param.18) | copy-start | bytes 12292
  97.6 2.7 %copy-start.3 = (f32[64,24,136]{2,1,0:T(8,128)S(1)}, f32[64,24,136]{2,1,0:T(8,128)}, u32[]{:S(2)}) copy-start(f32[64,24,136]{2,1,0:T(8,128)} %copy-done.2) | copy-start | bytes 2506756
  99.3 5.2 %slice-start = ((s8[7864320]{0:T(1024)(128)(4,1)}), s8[4194304]{0:T(1024)(128)(4,1)S(1)}, s32[]{:S(2)}) async-start(s8[7864320]{0:T(1024)(128)(4,1)} %bitcast.121), calls=%async_computation | async-start | bytes 8388608
  100.2 4.3 %slice-start.1 = ((s8[7864320]{0:T(1024)(128)(4,1)}), s8[3670016]{0:T(1024)(128)(4,1)S(1)}, s32[]{:S(2)}) async-start(s8[7864320]{0:T(1024)(128)(4,1)} %bitcast.121), calls=%async_computation.1 | async-start | bytes 7340032
  113.7 8.1 %copy-start.5 = (f32[64,24,136]{2,1,0:T(8,128)S(1)}, f32[64,24,136]{2,1,0:T(8,128)}, u32[]{:S(2)}) copy-start(f32[64,24,136]{2,1,0:T(8,128)} %copy-done.4) | copy-start | bytes 2506756
  114.5 5.6 %collective-permute-start.4 = (f32[65,24,4]{0,1,2:T(8,128)S(1)}, f32[65,24,4]{0,1,2:T(8,128)S(1)}, u32[]{:S(2)}, u32[]{:S(2)}) collective-permute-start(f32[65,24,4]{0,1,2:T(8,128)S(1)} %concatenate.84.clone), channel_id=1, source_target_pairs={{0,1},{1,2},{2,3},{3,4},{4,5},{5,6},{6,7},{7,8},{8,9},{9,10},{10,1... | collective-permute-start | bytes 74888 | tf_op jit(solution)/shard_map/ppermute | solution.py:54
  115.0 5.6 %collective-permute-start.5 = (f32[65,24,4]{0,1,2:T(8,128)S(1)}, f32[65,24,4]{0,1,2:T(8,128)S(1)}, u32[]{:S(2)}, u32[]{:S(2)}) collective-permute-start(f32[65,24,4]{0,1,2:T(8,128)S(1)} %concatenate.85.clone), channel_id=1, source_target_pairs={{1,0},{2,1},{3,2},{4,3},{5,4},{6,5},{7,6},{8,7},{9,8},{10,9},{11,1... | collective-permute-start | bytes 74888 | tf_op jit(solution)/shard_map/ppermute | solution.py:55
  123.3 9.9 %collective-permute-start.6 = (f32[65,4,128]{2,1,0:T(4,128)S(1)}, f32[65,4,128]{2,1,0:T(4,128)S(1)}, u32[]{:S(2)}, u32[]{:S(2)}) collective-permute-start(f32[65,4,128]{2,1,0:T(4,128)S(1)} %concatenate.86), channel_id=1, source_target_pairs={{0,16},{16,32},{32,48},{48,64},{64,80},{80,96},{96,112},{112,128},... | collective-permute-start | bytes 399368 | tf_op jit(solution)/shard_map/ppermute | solution.py:54
  125.3 9.8 %collective-permute-start.7 = (f32[65,4,128]{2,1,0:T(4,128)S(1)}, f32[65,4,128]{2,1,0:T(4,128)S(1)}, u32[]{:S(2)}, u32[]{:S(2)}) collective-permute-start(f32[65,4,128]{2,1,0:T(4,128)S(1)} %concatenate.87), channel_id=1, source_target_pairs={{16,0},{32,16},{48,32},{64,48},{80,64},{96,80},{112,96},{128,112},... | collective-permute-start | bytes 399368 | tf_op jit(solution)/shard_map/ppermute | solution.py:55
  136.9 5.0 %collective-permute-start.8 = (f32[]{:T(128)}, f32[]{:T(128)}, u32[]{:S(2)}, u32[]{:S(2)}) collective-permute-start(f32[]{:T(128)} %add.358), channel_id=1, source_target_pairs={{0,2},{1,3},{2,0},{3,1},{4,6},{5,7},{6,4},{7,5},{8,10},{9,11},{10,... | collective-permute-start | bytes 20 | tf_op jit(solution)/shard_map/ppermute | solution.py:76
  142.6 8.5 %collective-permute-start.9 = (f32[]{:T(128)}, f32[]{:T(128)}, u32[]{:S(2)}, u32[]{:S(2)}) collective-permute-start(f32[]{:T(128)} %add.359), channel_id=1, source_target_pairs={{0,4},{1,5},{2,6},{3,7},{4,0},{5,1},{6,2},{7,3},{8,12},{9,13},{10,... | collective-permute-start | bytes 20 | tf_op jit(solution)/shard_map/ppermute | solution.py:76
  151.7 7.5 %collective-permute-start.10 = (f32[]{:T(128)}, f32[]{:T(128)}, u32[]{:S(2)}, u32[]{:S(2)}) collective-permute-start(f32[]{:T(128)} %add.360), channel_id=1, source_target_pairs={{0,8},{1,9},{2,10},{3,11},{4,12},{5,13},{6,14},{7,15},{8,0},{9,1},... | collective-permute-start | bytes 20 | tf_op jit(solution)/shard_map/ppermute | solution.py:76
  159.8 3.6 %collective-permute-start.11 = (f32[]{:T(128)}, f32[]{:T(128)}, u32[]{:S(2)}, u32[]{:S(2)}) collective-permute-start(f32[]{:T(128)} %add.361), channel_id=1, source_target_pairs={{0,32},{16,48},{32,0},{48,16},{64,96},{80,112},{96,64},{112,80},{1... | collective-permute-start | bytes 20 | tf_op jit(solution)/shard_map/ppermute | solution.py:76
  164.0 5.1 %collective-permute-start.12 = (f32[]{:T(128)}, f32[]{:T(128)}, u32[]{:S(2)}, u32[]{:S(2)}) collective-permute-start(f32[]{:T(128)} %add.362), channel_id=1, source_target_pairs={{0,64},{16,80},{32,96},{48,112},{64,0},{80,16},{96,32},{112,48},{1... | collective-permute-start | bytes 20 | tf_op jit(solution)/shard_map/ppermute | solution.py:76
  169.8 5.1 %collective-permute-start.13 = (f32[]{:T(128)}, f32[]{:T(128)}, u32[]{:S(2)}, u32[]{:S(2)}) collective-permute-start(f32[]{:T(128)} %add.363), channel_id=1, source_target_pairs={{0,128},{16,144},{32,160},{48,176},{64,192},{80,208},{96,224},{112... | collective-permute-start | bytes 20 | tf_op jit(solution)/shard_map/ppermute | solution.py:76
  (8 other events, 11.2 us)
